TPU v7x, 128 devices: a whole 4x4x4 slice. The times are simulated.
128 devices in a mesh: dp: 32 (over x, z, core), fsdp: 4 (over y).
Axes of the slice: x: 4, y: 4, z: 4, core: 2. Of those that a mesh axis runs over, the one named last changes fastest.
Arguments:
- latents: bfloat16 [2816, 8, 8, 320], P(('dp', 'fsdp')), may hold values from -6 to 6
- noise_draw: bfloat16 [2816, 8, 8, 320], P(('dp', 'fsdp')), may hold values from -6 to 6
- timesteps: int32 [2816], P(('dp', 'fsdp')), may hold values from 0 to 999
- buckets: int32 [2816], P(('dp', 'fsdp')), may hold values from 0 to 2
- owners: int32 [2816], P(('dp', 'fsdp')), may hold values from 0 to 31, as said below
- adv_grad: bfloat16 [2816, 8, 8, 320], P(('dp', 'fsdp')), may hold values from -6 to 6
- w_down: bfloat16 [2880, 640], P('fsdp'), may hold values from -0.109375 to 0.109375
- w_up: bfloat16 [5760, 320], P('fsdp'), may hold values from -0.078125 to 0.078125
- t_down: bfloat16 [2880, 640], P('fsdp'), may hold values from -0.109375 to 0.109375
- t_up: bfloat16 [5760, 320], P('fsdp'), may hold values from -0.078125 to 0.078125
Outputs:
- student_out: bfloat16 [2816, 8, 8, 320], P(('dp', 'fsdp'))
- grad_down: float32 [2880, 640], P('fsdp')
- grad_up: float32 [5760, 320], P('fsdp')
Inputs may be any that keep to these rules, and one draw needn't show every extreme that they name: `owners`: within one index of fsdp every owner receives exactly 22 tiles; at most 2 of one device's tiles name the same owner, and on every device some owner is named exactly 2 times.
All inputs are finite; a program needn't handle non-finite values.
Results may differ from a plain program's by a relative error of at most 0.015.
Values may be sent and summed in bfloat16 or wider, within the bound.
No kernel may reach another device: no remote copies, remote signals or barrier semaphores. Data moves between devices by JAX's collectives and lax.ppermute only.
A program may use at most 320 MiB of HBM per device.

v0:
```python
import jax
import jax.numpy as jnp
from jax import lax
from jax.sharding import PartitionSpec as P

GROUPS = 32
TSTEPS = 1000
distill_weight = 2.5
norm_epsilon = 1e-05


def conv_forward(volume, kernel_rows, stride):
    in_chan = volume.shape[3]
    kernel = kernel_rows.reshape(3, 3, in_chan, kernel_rows.shape[1])
    return lax.conv_general_dilated(
        volume,
        kernel,
        (stride, stride),
        ((1, 1), (1, 1)),
        dimension_numbers=("NHWC", "HWIO", "NHWC"),
        preferred_element_type=jnp.float32,
    )


def kernel_grad(volume, cotangent, stride):
    pad_upper = 1 if stride == 1 else 0
    result_grad = lax.conv_general_dilated(
        volume,
        cotangent,
        (1, 1),
        ((1, pad_upper), (1, pad_upper)),
        rhs_dilation=(stride, stride),
        dimension_numbers=("CHWN", "IHWO", "HWNC"),
        preferred_element_type=jnp.float32,
    )
    return result_grad.reshape(9 * volume.shape[3], cotangent.shape[3])


def width_masks(buckets, tile_side):
    half_side = tile_side // 2
    tile_count = buckets.shape[0]
    columns = jnp.arange(tile_side, dtype=jnp.int32)
    full_mask = (
        columns[None, None, :, None] < (tile_side - 2 * buckets)[:, None, None, None]
    ).astype(jnp.float32)
    full_mask = jnp.broadcast_to(full_mask, (tile_count, tile_side, tile_side, 1))
    half_cols = jnp.arange(half_side, dtype=jnp.int32)
    half_mask = (
        half_cols[None, None, :, None] < (half_side - buckets)[:, None, None, None]
    ).astype(jnp.float32)
    half_mask = jnp.broadcast_to(half_mask, (tile_count, half_side, half_side, 1))
    return (full_mask, half_mask)


def group_stats(hidden, half_mask):
    tile_count, height, breadth, channels = hidden.shape
    grouped = hidden.reshape(tile_count, height * breadth, GROUPS, channels // GROUPS)
    live_weight = half_mask.reshape(tile_count, height * breadth, 1, 1)
    population = jnp.sum(live_weight, axis=(1, 3), keepdims=True) * (channels // GROUPS)
    center = jnp.sum(grouped * live_weight, axis=(1, 3), keepdims=True) / population
    spread = (
        jnp.sum(jnp.square(grouped - center) * live_weight, axis=(1, 3), keepdims=True) / population
    )
    inverse = lax.rsqrt(spread + norm_epsilon)
    normed = ((grouped - center) * inverse).reshape(hidden.shape)
    return (normed, inverse, population)


def group_back(d_norm, normed, inverse, population, half_mask):
    tile_count, height, breadth, channels = d_norm.shape
    grouped_d = d_norm.reshape(tile_count, height * breadth, GROUPS, channels // GROUPS)
    grouped_n = normed.reshape(tile_count, height * breadth, GROUPS, channels // GROUPS)
    live_weight = half_mask.reshape(tile_count, height * breadth, 1, 1)
    mean_first = jnp.sum(grouped_d, axis=(1, 3), keepdims=True) / population
    mean_second = jnp.sum(grouped_d * grouped_n, axis=(1, 3), keepdims=True) / population
    result = live_weight * inverse * (grouped_d - mean_first - grouped_n * mean_second)
    return result.reshape(d_norm.shape)


def upsample(activated):
    return jnp.repeat(jnp.repeat(activated, 2, axis=1), 2, axis=2)


def network(noisy, full_mask, half_mask, down_weight, up_weight):
    hidden = conv_forward(noisy, down_weight, 2)
    normed, inverse, population = group_stats(hidden, half_mask)
    activated = (half_mask * jax.nn.silu(normed)).astype(jnp.bfloat16)
    enlarged = upsample(activated)
    output = conv_forward(enlarged, up_weight, 1)
    student = (full_mask * (noisy.astype(jnp.float32) + output)).astype(jnp.bfloat16)
    return (student, (noisy, normed, inverse, population, activated, enlarged))


def flip_kernel(up_weight):
    up_chan = up_weight.shape[0] // 9
    out_chan = up_weight.shape[1]
    return (
        up_weight.reshape(3, 3, up_chan, out_chan)[::-1, ::-1]
        .transpose(0, 1, 3, 2)
        .reshape(9 * out_chan, up_chan)
    )


def cotangents(student, target, adversarial, full_mask, half_mask, flipped, cached, loss_scale):
    source_in, normed, inverse, population, activated, enlarged = cached
    tile_count, tile_side = (student.shape[0], student.shape[1])
    half_side = tile_side // 2
    d_out = (
        full_mask
        * (
            distill_weight * (student.astype(jnp.float32) - target.astype(jnp.float32))
            + adversarial.astype(jnp.float32)
        )
        * loss_scale
    ).astype(jnp.bfloat16)
    d_up = conv_forward(d_out, flipped, 1)
    d_up = d_up.reshape(tile_count, half_side, 2, half_side, 2, flipped.shape[1])
    d_act = jnp.sum(d_up, axis=(2, 4))
    sigmoid_n = jax.nn.sigmoid(normed)
    d_norm = half_mask * d_act * sigmoid_n * (1.0 + normed * (1.0 - sigmoid_n))
    d_hidden = group_back(d_norm, normed, inverse, population, half_mask).astype(jnp.bfloat16)
    return (d_out, d_hidden)


def on_device(
    latents, noise_draw, timesteps, buckets, owners, adv_grad, w_down, w_up, t_down, t_up
):
    tile_count, tile_side = (latents.shape[0], latents.shape[1])
    dp_count = lax.axis_size("dp")
    fsdp_count = lax.axis_size("fsdp")
    full_mask, half_mask = width_masks(buckets, tile_side)
    alpha_bar = jnp.square(jnp.cos(0.5 * jnp.pi * (timesteps.astype(jnp.float32) + 0.5) / TSTEPS))
    noisy = (
        full_mask
        * (
            jnp.sqrt(alpha_bar)[:, None, None, None] * latents.astype(jnp.float32)
            + jnp.sqrt(1.0 - alpha_bar)[:, None, None, None] * noise_draw.astype(jnp.float32)
        )
    ).astype(jnp.bfloat16)
    peer_cap = max(2, (tile_count + dp_count - 1) // dp_count)
    slot_count = dp_count * peer_cap
    hit_table = (owners[:, None] == jnp.arange(dp_count, dtype=jnp.int32)[None, :]).astype(
        jnp.int32
    )
    before = jnp.cumsum(hit_table, axis=0) - hit_table
    slot_of = owners * peer_cap + jnp.sum(before * hit_table, axis=1)
    slot_hits = slot_of[None, :] == jnp.arange(slot_count, dtype=jnp.int32)[:, None]
    spread_matrix = slot_hits.astype(jnp.bfloat16)
    send_noisy = (
        jnp.dot(spread_matrix, noisy.reshape(tile_count, -1), preferred_element_type=jnp.float32)
        .astype(jnp.bfloat16)
        .reshape(dp_count, peer_cap, -1)
    )
    send_code = jnp.sum(jnp.where(slot_hits, buckets[None, :] + 1, 0), axis=1).reshape(
        dp_count, peer_cap
    )
    teacher_down, teacher_up = (
        lax.all_gather(t_down, "fsdp", axis=0, tiled=True),
        lax.all_gather(t_up, "fsdp", axis=0, tiled=True),
    )
    recv_noisy, recv_code = (
        lax.all_to_all(send_noisy, "dp", split_axis=0, concat_axis=0, tiled=True),
        lax.all_to_all(send_code, "dp", split_axis=0, concat_axis=0, tiled=True),
    )
    flat_code = recv_code.reshape(slot_count)
    live_slot = (flat_code > 0).astype(jnp.int32)
    position = jnp.cumsum(live_slot) - live_slot
    pick_hits = (live_slot[None, :] == 1) & (
        position[None, :] == jnp.arange(tile_count, dtype=jnp.int32)[:, None]
    )
    pick_matrix = pick_hits.astype(jnp.bfloat16)
    own_noisy = (
        jnp.dot(pick_matrix, recv_noisy.reshape(slot_count, -1), preferred_element_type=jnp.float32)
        .astype(jnp.bfloat16)
        .reshape(latents.shape)
    )
    own_buckets = jnp.sum(jnp.where(pick_hits, flat_code[None, :] - 1, 0), axis=1).astype(jnp.int32)
    own_full, own_half = width_masks(own_buckets, tile_side)
    student_down, student_up = (
        lax.all_gather(w_down, "fsdp", axis=0, tiled=True),
        lax.all_gather(w_up, "fsdp", axis=0, tiled=True),
    )
    student, cached = network(own_noisy, own_full, own_half, student_down, student_up)
    target, _ = network(own_noisy, own_full, own_half, teacher_down, teacher_up)
    loss_scale = jnp.float32(1.0 / (tile_count * dp_count * fsdp_count))
    flipped = flip_kernel(student_up)
    d_out, d_hidden = cotangents(
        student, target, adv_grad, own_full, own_half, flipped, cached, loss_scale
    )
    local_down = kernel_grad(cached[0], d_hidden, 2)
    local_up = kernel_grad(cached[5], d_out, 1)
    shard_down, shard_up = (
        lax.psum_scatter(
            local_down.astype(jnp.bfloat16), "fsdp", scatter_dimension=0, tiled=True
        ).astype(jnp.float32),
        lax.psum_scatter(
            local_up.astype(jnp.bfloat16), "fsdp", scatter_dimension=0, tiled=True
        ).astype(jnp.float32),
    )
    grad_down, grad_up = (
        lax.psum(shard_down.astype(jnp.bfloat16), "dp").astype(jnp.float32),
        lax.psum(shard_up.astype(jnp.bfloat16), "dp").astype(jnp.float32),
    )
    return (student, grad_down, grad_up)


def solution(mesh):
    return jax.shard_map(
        on_device,
        mesh=mesh,
        in_specs=(
            P(("dp", "fsdp"), None, None, None),
            P(("dp", "fsdp"), None, None, None),
            P(("dp", "fsdp")),
            P(("dp", "fsdp")),
            P(("dp", "fsdp")),
            P(("dp", "fsdp"), None, None, None),
            P("fsdp", None),
            P("fsdp", None),
            P("fsdp", None),
            P("fsdp", None),
        ),
        out_specs=(P(("dp", "fsdp"), None, None, None), P("fsdp", None), P("fsdp", None)),
        check_vma=False,
    )
```

profile of v0, /device:TPU:1, one launch (start us, length us, event | category | flops | bytes accessed | tf_op | source)
XLA Modules:
  0.0 477.1 jit_solution(6874258647348290337)
XLA Ops:
  10.6 9.4 %all-to-all-start = ((s32[32,1,2]{2,1,0:T(1,128)}), s32[32,1,2]{2,1,0:T(1,128)S(1)}, u32[]{:S(2)}, u32[]{:S(2)}) async-start(s32[32,1,2]{2,1,0:T(1,128)} %bitcast), calls=%async_computation | async-start | bytes 32768 | tf_op jit(solution)/shard_map/all_to_all | solution.py:163
  20.9 2.2 reshape.386
  23.1 2.2 convolution_convert_fusion
  25.3 3.0 reshape.387
  28.3 7.4 %all-to-all-start.1 = ((bf16[32,2,20480]{2,1,0:T(2,128)(2,1)}), bf16[32,2,20480]{2,1,0:T(2,128)(2,1)S(1)}, u32[]{:S(2)}, u32[]{:S(2)}) async-start(bf16[32,2,20480]{2,1,0:T(2,128)(2,1)} %reshape.387), calls=%async_computation.1 | async-start | bytes 5242880 | tf_op jit(solution)/shard_map/all_to_all | solution.py:162
  38.9 30.7 %all-to-all-done.1 = bf16[32,2,20480]{2,1,0:T(2,128)(2,1)S(1)} async-done(((bf16[32,2,20480]{2,1,0:T(2,128)(2,1)}), bf16[32,2,20480]{2,1,0:T(2,128)(2,1)S(1)}, u32[]{:S(2)}, u32[]{:S(2)}) %all-to-all-start.1) | async-done | bytes 2621472 | tf_op jit(solution)/shard_map/all_to_all | solution.py:162
  69.6 2.4 reshape.388
  72.1 2.2 convolution_convert_fusion.1
  74.3 1.3 reshape.389
  75.6 5.3 %fusion.8 = f32[22,4,4,640]{3,0,2,1:T(8,128)S(1)} fusion(bf16[3,3,320,640]{3,2,1,0:T(8,128)(2,1)} %bitcast.49, bf16[22,8,8,320]{3,2,1,0:T(8,128)(2,1)S(1)} %reshape.389), kind=kOutput, calls=%fused_computation.27 | convolution fusion | flops 1090355200 | bytes 5488640 | tf_op jit(solution)/shard_map/conv_general_dilated | solution.py:15
  80.9 21.8 %all-gather.9.cloned.1.call-done = bf16[2880,640]{1,0:T(8,128)(2,1)} async-done(((bf16[720,640]{1,0:T(8,128)(2,1)}), bf16[2880,640]{1,0:T(8,128)(2,1)}) %all-gather.9.cloned.1.call-update) | async-done | bytes 3686416 | tf_op jit(solution)/shard_map/all_gather | solution.py:158
  102.7 5.0 %multiply_reduce_fusion.2 = (f32[22,640]{1,0:T(8,128)S(1)}, f32[22,640]{1,0:T(8,128)S(1)}, f32[22,4,4,640]{3,0,2,1:T(8,128)S(1)}) fusion(f32[22,4]{0,1:T(4,128)S(1)} %fusion.23, f32[22,4,4,640]{3,0,2,1:T(8,128)S(1)} %fusion.8, bf16[3,3,320,640]{3,2,1,0:T(8,128)(2,1)} %bitcast.50, bf16[22,8,8,320]{3,2,1,0:T(8,128)(2,1)S(1)} %reshape.389), kind=kOutput, calls=%fused_computation.18 | convolution fusion | flops 1091228160 | bytes 6502752 | tf_op jit(solution)/shard_map/conv_general_dilated | solution.py:15
  111.4 0.8 mul.206
  112.4 0.8 mul.220
  113.2 37.4 %all-gather.11.cloned.1.call-done = bf16[4,1440,320]{1,2,0:T(8,128)(2,1)} async-done(((bf16[1,1440,320]{1,2,0:T(8,128)(2,1)}), bf16[4,1440,320]{1,2,0:T(8,128)(2,1)}) %all-gather.11.cloned.1.call-update) | async-done | bytes 3686416 | tf_op jit(solution)/shard_map/all_gather | solution.py:181
  150.7 6.5 %copy.64 = bf16[4,1440,320]{2,1,0:T(8,128)(2,1)} copy(bf16[4,1440,320]{1,2,0:T(8,128)(2,1)} %all-gather.11.cloned.1.call-done) | data formatting | bytes 7372800 | tf_op jit(solution)/shard_map/all_gather | solution.py:181
  157.2 1.6 multiply_convert_fusion.2
  159.1 1.3 copy-done.2
  160.4 1.5 copy-done
  161.8 11.1 %fusion.1 = bf16[22,8,8,320]{3,0,2,1:T(8,128)(2,1)} fusion(bf16[22,8,8,640]{3,0,2,1:T(8,128)(2,1)S(1)} %bitcast.42, bf16[3,3,640,320]{3,2,1,0:T(8,128)(2,1)S(1)} %bitcast.33, f32[22,8]{0,1:T(8,128)S(1)} %copy-done.19, bf16[22,8,8,320]{3,2,1,0:T(8,128)(2,1)S(1)} %copy-done.8), kind=kOutput, calls=%fused_computation.7 | convolution fusion | flops 4363223040 | bytes 7291584 | tf_op jit(solution)/shard_map/conv_general_dilated | solution.py:15
  172.9 25.6 %all-gather.13.cloned.1.call-done = bf16[4,1440,320]{1,2,0:T(8,128)(2,1)} async-done(((bf16[1,1440,320]{1,2,0:T(8,128)(2,1)}), bf16[4,1440,320]{1,2,0:T(8,128)(2,1)}) %all-gather.13.cloned.1.call-update) | async-done | bytes 3686416 | tf_op jit(solution)/shard_map/all_gather | solution.py:159
  198.5 6.3 %copy.67 = bf16[4,1440,320]{2,1,0:T(8,128)(2,1)} copy(bf16[4,1440,320]{1,2,0:T(8,128)(2,1)} %all-gather.13.cloned.1.call-done) | data formatting | bytes 7372800 | tf_op jit(solution)/shard_map/all_gather | solution.py:159
  205.2 1.9 copy-done.1
  207.2 12.3 %multiply_convert_fusion = bf16[22,8,8,320]{3,0,2,1:T(8,128)(2,1)S(1)} fusion(bf16[22,8,8,320]{3,0,2,1:T(8,128)(2,1)} %fusion.1, bf16[22,8,8,640]{3,0,2,1:T(8,128)(2,1)S(1)} %bitcast.44, bf16[3,3,640,320]{3,2,1,0:T(8,128)(2,1)S(1)} %bitcast.37, bf16[22,8,8,320]{3,2,1,0:T(8,128)(2,1)} %param.15, f32[22,8]{0,1:T(8,128)S(1)} %copy-done.19, ...), kind=kOutput, calls=%fused_computation.10 | convolution fusion | flops 4367278080 | bytes 9093824 | tf_op jit(solution)/shard_map/conv_general_dilated | solution.py:15
  219.5 10.7 %fusion.27 = f32[22,8,8,640]{3,0,2,1:T(8,128)} fusion(bf16[22,8,8,320]{3,0,2,1:T(8,128)(2,1)S(1)} %multiply_convert_fusion, bf16[3,3,640,320]{3,2,1,0:T(8,128)(2,1)S(1)} %bitcast.36), kind=kOutput, calls=%fused_computation.72 | convolution fusion | flops 4361420800 | bytes 8192000 | tf_op jit(solution)/shard_map/conv_general_dilated | solution.py:15
  230.3 2.5 reduce_sum.161
  232.8 1.2 fusion.26
  233.9 1.2 reduce_sum.163
  235.2 0.8 reduce_sum.164
  235.9 1.2 reduce_sum.166
  237.2 0.8 reduce_sum.167
  237.9 1.4 broadcast_divide_fusion.1
  239.5 0.8 mul.237
  240.3 0.9 sub.114
  241.2 0.8 sub.115
  242.1 0.8 broadcast_multiply_fusion
  242.9 3.6 mul.215
  246.5 7.6 %mul.216 = f32[22,4,4,640]{3,2,1,0:T(4,128)} reshape(f32[22,16,32,20]{3,2,1,0:T(8,128)} %mul.215) | data formatting | bytes 1802240 | tf_op jit(solution)/shard_map/mul | solution.py:76
  254.1 6.4 %convolution_convert_fusion.2 = bf16[3,3,320,640]{3,2,1,0:T(8,128)(2,1)} fusion(bf16[22,8,8,320]{3,2,1,0:T(8,128)(2,1)S(1)} %copy-done.8, f32[22,4,4,640]{3,2,1,0:T(4,128)} %mul.216, f32[22,4,4,640]{3,0,2,1:T(8,128)S(1)} %fusion.8, f32[22,640]{1,0:T(8,128)S(1)} %copy-done.14, f32[22,640]{1,0:T(8,128)S(1)} %copy-done.15, f32[22,640]{1,0:T(8,128)S(1)} %copy-done.12, ...), kind=kOutput, calls=%fused_computation.4 | convolution fusion | flops 1095802880 | bytes 7516512 | tf_op jit(solution)/shard_map/conv_general_dilated | solution.py:27
  260.6 1.5 copy-done.3
  262.4 7.9 %convolution_convert_fusion.3 = bf16[3,3,640,320]{2,3,1,0:T(8,128)(2,1)} fusion(bf16[22,8,8,640]{3,0,2,1:T(8,128)(2,1)S(1)} %bitcast.43, bf16[22,8,8,320]{3,0,2,1:T(8,128)(2,1)S(1)} %copy-done.23), kind=kOutput, calls=%fused_computation.5 | convolution fusion | flops 4363264000 | bytes 6389760 | tf_op jit(solution)/shard_map/conv_general_dilated | solution.py:27
  270.3 7.9 %copy.71 = bf16[3,3,640,320]{3,2,1,0:T(8,128)(2,1)} copy(bf16[3,3,640,320]{2,3,1,0:T(8,128)(2,1)} %convolution_convert_fusion.3) | data formatting | bytes 7372800 | tf_op jit(solution)/shard_map/convert_element_type | solution.py:197
  278.3 25.7 %reduce-scatter.3.cloned.1.call-done = bf16[720,640]{1,0:T(8,128)(2,1)} async-done(((bf16[2880,640]{1,0:T(8,128)(2,1)}), bf16[720,640]{1,0:T(8,128)(2,1)}) %reduce-scatter.3.cloned.1.call-update) | async-done | bytes 921616 | tf_op jit(solution)/shard_map/reduce_scatter | solution.py:193
  303.9 50.8 %reduce-scatter.5.cloned.1.call-done = bf16[1440,320]{1,0:T(8,128)(2,1)} async-done(((bf16[5760,320]{1,0:T(8,128)(2,1)}), bf16[1440,320]{1,0:T(8,128)(2,1)}) %reduce-scatter.5.cloned.1.call-update) | async-done | bytes 921616 | tf_op jit(solution)/shard_map/reduce_scatter | solution.py:196
  354.7 1.2 copy.72
  355.9 110.0 %all-reduce.3.cloned.1.call-done = (bf16[1440,320]{1,0:T(8,128)(2,1)}, bf16[720,640]{1,0:T(8,128)(2,1)}) async-done(((bf16[1440,320]{1,0:T(8,128)(2,1)}, bf16[720,640]{1,0:T(8,128)(2,1)}), (bf16[1440,320]{1,0:T(8,128)(2,1)}, bf16[720,640]{1,0:T(8,128)(2,1)})) %all-reduce.3.cloned.1.call-update) | async-done | bytes 1843216 | tf_op jit(solution)/shard_map/psum | solution.py:202
  465.9 2.6 copy.73
  468.5 1.4 convert_element_type.153
  (113 shorter events, 12.4 us)
Async XLA Ops:
  7.2 2.3 copy-start.18
  7.2 2.6 copy-start.20
  7.2 12.8 %copy-start.21 = (s32[22]{0:T(128)S(1)}, s32[22]{0:T(128)}, u32[]{:S(2)}) copy-start(s32[22]{0:T(128)} %param.12) | copy-start | bytes 268
  7.2 12.9 %copy-start.6 = (bf16[22,8,8,320]{3,2,1,0:T(8,128)(2,1)S(1)}, bf16[22,8,8,320]{3,2,1,0:T(8,128)(2,1)}, u32[]{:S(2)}) copy-start(bf16[22,8,8,320]{3,2,1,0:T(8,128)(2,1)} %param.10) | copy-start | bytes 2703364
  7.2 12.9 %copy-start.5 = (bf16[22,8,8,320]{3,2,1,0:T(8,128)(2,1)S(1)}, bf16[22,8,8,320]{3,2,1,0:T(8,128)(2,1)}, u32[]{:S(2)}) copy-start(bf16[22,8,8,320]{3,2,1,0:T(8,128)(2,1)} %param.11) | copy-start | bytes 2703364
  7.2 68.4 %all-gather.7.cloned.1.call-start = ((), (), s32[]{:S(2)}) async-start(), calls=%async_computation.4 | async-start | bytes 4608000 | tf_op jit(solution)/shard_map/all_gather | solution.py:180
  7.9 94.7 %all-gather.9.cloned.1.call-start = ((), (), s32[]{:S(2)}) async-start(), calls=%async_computation.5 | async-start | bytes 4608000 | tf_op jit(solution)/shard_map/all_gather | solution.py:158
  8.7 142.0 %all-gather.11.cloned.1.call-start = ((), (), s32[]{:S(2)}) async-start(), calls=%async_computation.8 | async-start | bytes 4915200 | tf_op jit(solution)/shard_map/all_gather | solution.py:181
  10.6 17.7 %all-to-all-start = ((s32[32,1,2]{2,1,0:T(1,128)}), s32[32,1,2]{2,1,0:T(1,128)S(1)}, u32[]{:S(2)}, u32[]{:S(2)}) async-start(s32[32,1,2]{2,1,0:T(1,128)} %bitcast), calls=%async_computation | async-start | bytes 32768 | tf_op jit(solution)/shard_map/all_to_all | solution.py:163
  28.3 41.3 %all-to-all-start.1 = ((bf16[32,2,20480]{2,1,0:T(2,128)(2,1)}), bf16[32,2,20480]{2,1,0:T(2,128)(2,1)S(1)}, u32[]{:S(2)}, u32[]{:S(2)}) async-start(bf16[32,2,20480]{2,1,0:T(2,128)(2,1)} %reshape.387), calls=%async_computation.1 | async-start | bytes 5242880 | tf_op jit(solution)/shard_map/all_to_all | solution.py:162
  35.7 162.9 %all-gather.13.cloned.1.call-start = ((), (), s32[]{:S(2)}) async-start(), calls=%async_computation.9 | async-start | bytes 4915200 | tf_op jit(solution)/shard_map/all_gather | solution.py:159
  36.3 267.6 %reduce-scatter.3.cloned.1.call-start = ((), (), s32[]{:S(2)}) async-start(), calls=%async_computation.6 | async-start | bytes 4608000 | tf_op jit(solution)/shard_map/reduce_scatter | solution.py:193
  38.3 72.8 %copy-start.16 = (f32[22]{0:T(128)}, f32[22]{0:T(128)S(1)}, u32[]{:S(2)}) copy-start(f32[22]{0:T(128)S(1)} %broadcast_multiply_fusion.1) | copy-start | bytes 268
  75.6 27.1 %copy-start.7 = (bf16[22,8,8,320]{3,2,1,0:T(8,128)(2,1)}, bf16[22,8,8,320]{3,2,1,0:T(8,128)(2,1)S(1)}, u32[]{:S(2)}) copy-start(bf16[22,8,8,320]{3,2,1,0:T(8,128)(2,1)S(1)} %reshape.389) | copy-start | bytes 2703364
  109.3 1.9 copy-start.9
  109.7 2.6 copy-start.13
  157.2 3.2 copy-start.8
  158.8 3.1 copy-start
  158.8 3.1 copy-start.19
  159.1 1.3 copy-start.2
  204.9 2.3 copy-start.1
  205.0 14.5 %slice-start = ((s8[4423680]{0:T(1024)(128)(4,1)}), s8[4194304]{0:T(1024)(128)(4,1)S(1)}, s32[]{:S(2)}) async-start(s8[4423680]{0:T(1024)(128)(4,1)} %bitcast.34), calls=%async_computation.11 | async-start | bytes 8388608
  207.2 12.4 %slice-start.1 = ((s8[4423680]{0:T(1024)(128)(4,1)}), s8[229376]{0:T(1024)(128)(4,1)S(1)}, s32[]{:S(2)}) async-start(s8[4423680]{0:T(1024)(128)(4,1)} %bitcast.34), calls=%async_computation.12 | async-start | bytes 458752
  219.5 10.8 %copy-start.22 = (bf16[22,8,8,320]{3,0,2,1:T(8,128)(2,1)}, bf16[22,8,8,320]{3,0,2,1:T(8,128)(2,1)S(1)}, u32[]{:S(2)}) copy-start(bf16[22,8,8,320]{3,0,2,1:T(8,128)(2,1)S(1)} %multiply_convert_fusion) | copy-start | bytes 2703364
  230.3 2.5 copy-start.10
  230.3 2.5 copy-start.12
  232.8 5.2 %copy-start.17 = (f32[22]{0:T(128)S(1)}, f32[22]{0:T(128)}, u32[]{:S(2)}) copy-start(f32[22]{0:T(128)} %copy-done.16) | copy-start | bytes 268
  246.5 7.7 %copy-start.14 = (f32[22,640]{1,0:T(8,128)S(1)}, f32[22,640]{1,0:T(8,128)}, u32[]{:S(2)}) copy-start(f32[22,640]{1,0:T(8,128)} %mul.237) | copy-start | bytes 168964
  246.5 7.7 %copy-start.15 = (f32[22,640]{1,0:T(8,128)S(1)}, f32[22,640]{1,0:T(8,128)}, u32[]{:S(2)}) copy-start(f32[22,640]{1,0:T(8,128)} %sub.115) | copy-start | bytes 168964
  260.6 1.5 copy-start.3
  260.6 1.9 copy-start.23
  260.6 94.1 %reduce-scatter.5.cloned.1.call-start = ((), (), s32[]{:S(2)}) async-start(), calls=%async_computation.7 | async-start | bytes 5529600 | tf_op jit(solution)/shard_map/reduce_scatter | solution.py:196
  278.2 76.5 %copy-start.4 = (bf16[22,8,8,320]{3,0,2,1:T(8,128)(2,1)S(1)}, bf16[22,8,8,320]{3,0,2,1:T(8,128)(2,1)}, u32[]{:S(2)}) copy-start(bf16[22,8,8,320]{3,0,2,1:T(8,128)(2,1)} %fusion.1) | copy-start | bytes 2703364
  278.2 187.7 %all-reduce.3.cloned.1.call-start = ((), (), s32[]{:S(2)}) async-start(), calls=%async_computation.10 | async-start | bytes 4055040 | tf_op jit(solution)/shard_map/psum | solution.py:202
  465.9 2.6 copy-start.11
Sparse Core Ops, SparseCore 0:
  9.7 47.0 all-gather.6
  58.4 44.2 all-gather.8
  104.4 46.2 all-gather.10
  152.2 46.3 all-gather.12
  260.7 43.1 reduce-scatter.2
  306.2 48.4 reduce-scatter.4
  358.1 107.6 all-reduce.2
where the time goes:
time: 482 us; the launch traced here: 477 us
  waiting for transfers between devices  305 us (63%)
  matrix products  63.2 us (13%)
  local copies, waits for them, and re-layouts  62.9 us (13%)
  starting transfers between devices  17.6 us (4%)
  between operations  15.1 us (3%)
  other arithmetic  13.8 us (3%)
    psum x1, waiting for transfers between devices, on_device(): lax.psum(shard_up.astype(jnp.bfloat16), 'dp').astype(jnp.float32)  110 us
    reduce_scatter x1, waiting for transfers between devices, on_device(): lax.psum_scatter(local_up.astype(jnp.bfloat16), 'fsdp', scatter_dimension...  50.8 us
    conv_general_dilated x5, matrix products, conv_forward(): lax.conv_general_dilated(volume, kernel, (stride, stride), ((1, 1), (1, 1...  44.4 us
    all_gather x1, waiting for transfers between devices, on_device(): lax.all_gather(w_up, 'fsdp', axis=0, tiled=True)  37.4 us
    all_to_all x1, waiting for transfers between devices, on_device(): lax.all_to_all(send_noisy, 'dp', split_axis=0, concat_axis=0, tiled=True)  30.7 us
    reduce_scatter x1, waiting for transfers between devices, on_device(): lax.psum_scatter(local_down.astype(jnp.bfloat16), 'fsdp', scatter_dimensi...  25.7 us
    all_gather x1, waiting for transfers between devices, on_device(): lax.all_gather(t_up, 'fsdp', axis=0, tiled=True)  25.6 us
    all_gather x1, waiting for transfers between devices, on_device(): lax.all_gather(t_down, 'fsdp', axis=0, tiled=True)  21.8 us
  transfers between devices with their start and end apart: 9, of which 7 were waited for; matrix products, arithmetic and copies ran while one was open for 14% of the time, Pallas kernels for 0%

commit v1 on v0

--- a/solution.py
+++ b/solution.py
@@ -7,6 +7,22 @@
 TSTEPS = 1000
 distill_weight = 2.5
 norm_epsilon = 1e-05
+
+
+def ring_gather(x, axis, dim):
+    ways, here, step = (lax.axis_size(axis), lax.axis_index(axis), x.shape[dim])
+    dims = [n * ways if d == dim else n for d, n in enumerate(x.shape)]
+    full = lax.dynamic_update_slice_in_dim(jnp.zeros(dims, x.dtype), x, here * step, axis=dim)
+    going_up = going_down = x
+    for far in range(1, ways // 2 + 1):
+        going_up = lax.ppermute(going_up, axis, [(d, (d + 1) % ways) for d in range(ways)])
+        full = lax.dynamic_update_slice_in_dim(full, going_up, (here - far) % ways * step, axis=dim)
+        if 2 * far < ways:
+            going_down = lax.ppermute(going_down, axis, [(d, (d - 1) % ways) for d in range(ways)])
+            full = lax.dynamic_update_slice_in_dim(
+                full, going_down, (here + far) % ways * step, axis=dim
+            )
+    return full
 
 
 def conv_forward(volume, kernel_rows, stride):
@@ -155,7 +171,7 @@
         dp_count, peer_cap
     )
     teacher_down, teacher_up = (
-        lax.all_gather(t_down, "fsdp", axis=0, tiled=True),
+        ring_gather(t_down, "fsdp", 0),
         lax.all_gather(t_up, "fsdp", axis=0, tiled=True),
     )
     recv_noisy, recv_code = (

time: 482 us -> 464 us (0.963)
  waiting for transfers between devices: 305 us -> 259 us
  local copies, waits for them, and re-layouts: 62.9 us -> 75.6 us
  other arithmetic: 13.8 us -> 23.7 us
    ppermute x0 -> x3, waiting for transfers between devices: none -> 52.5 us  [the longest x2 52.5 us: ring_gather(): lax.ppermute(going_up, axis, [(d, (d + 1) % ways) for d in range(ways)])]
    all_gather x1, waiting for transfers between devices: 37.4 us -> 0.01 us  [on_device(): lax.all_gather(w_up, 'fsdp', axis=0, tiled=True)]
    all_to_all x1, waiting for transfers between devices: 30.7 us -> 0.01 us  [on_device(): lax.all_to_all(send_noisy, 'dp', split_axis=0, concat_axis=0, tiled=True)]
    all_gather x1 -> x0, waiting for transfers between devices: 21.8 us -> none  [on_device(): lax.all_gather(t_down, 'fsdp', axis=0, tiled=True)]
    dynamic_update_slice x0 -> x4, local copies, waits for them, and re-layouts: none -> 7.77 us  [the longest x2 4.47 us: ring_gather(): lax.dynamic_update_slice_in_dim(full, going_up, (here - far) % ways * ste...]
    all_gather x1, waiting for transfers between devices: 25.6 us -> 18.2 us  [on_device(): lax.all_gather(t_up, 'fsdp', axis=0, tiled=True)]
    unnamed x54 -> x58, local copies, waits for them, and re-layouts: 10.4 us -> 10.3 us
  transfers between devices with their start and end apart: 9 -> 11, of which waited for: 7 -> 6; matrix products, arithmetic and copies ran while one was open for 14% -> 20% of each run, Pallas kernels for 0% -> 0%
where the time goes in v1:
time: 464 us; the launch traced here: 457 us
  waiting for transfers between devices  259 us (56%)
  local copies, waits for them, and re-layouts  75.6 us (16%)
  matrix products  63.3 us (14%)
  other arithmetic  23.7 us (5%)
  starting transfers between devices  20.3 us (4%)
  between operations  14.9 us (3%)
    psum x1, waiting for transfers between devices, on_device(): lax.psum(shard_up.astype(jnp.bfloat16), 'dp').astype(jnp.float32)  110 us
    ppermute x2, waiting for transfers between devices, ring_gather(): lax.ppermute(going_up, axis, [(d, (d + 1) % ways) for d in range(ways)])  52.5 us
    reduce_scatter x1, waiting for transfers between devices, on_device(): lax.psum_scatter(local_up.astype(jnp.bfloat16), 'fsdp', scatter_dimension...  50.7 us
    conv_general_dilated x5, matrix products, conv_forward(): lax.conv_general_dilated(volume, kernel, (stride, stride), ((1, 1), (1, 1...  44.6 us
    reduce_scatter x1, waiting for transfers between devices, on_device(): lax.psum_scatter(local_down.astype(jnp.bfloat16), 'fsdp', scatter_dimensi...  25.7 us
    all_gather x1, waiting for transfers between devices, on_device(): lax.all_gather(t_up, 'fsdp', axis=0, tiled=True)  18.2 us
    conv_general_dilated x2, matrix products, kernel_grad(): lax.conv_general_dilated(volume, cotangent, (1, 1), ((1, pad_upper), (1,...  14.3 us
    mul x2, local copies, waits for them, and re-layouts, group_back(): live_weight * inverse * (grouped_d - mean_first - grouped_n * mean_second)  11.2 us
  transfers between devices with their start and end apart: 11, of which 6 were waited for; matrix products, arithmetic and copies ran while one was open for 20% of the time, Pallas kernels for 0%

profile of v1, /device:TPU:1, one launch (start us, length us, event | category | flops | bytes accessed | tf_op | source)
XLA Modules:
  0.0 456.9 jit_solution(13810616990987108178)
XLA Ops:
  11.8 9.5 %all-to-all-start = ((s32[32,1,2]{2,1,0:T(1,128)}), s32[32,1,2]{2,1,0:T(1,128)}, u32[]{:S(2)}, u32[]{:S(2)}) async-start(s32[32,1,2]{2,1,0:T(1,128)} %bitcast), calls=%async_computation | async-start | bytes 32768 | tf_op jit(solution)/shard_map/all_to_all | solution.py:179
  22.0 2.1 multiply_convert_fusion.1
  24.1 2.2 reshape.386
  26.3 2.1 convolution_convert_fusion
  28.5 3.0 reshape.387
  31.5 7.5 %all-to-all-start.1 = ((bf16[32,2,20480]{2,1,0:T(2,128)(2,1)}), bf16[32,2,20480]{2,1,0:T(2,128)(2,1)S(1)}, u32[]{:S(2)}, u32[]{:S(2)}) async-start(bf16[32,2,20480]{2,1,0:T(2,128)(2,1)} %reshape.387), calls=%async_computation.1 | async-start | bytes 5242880 | tf_op jit(solution)/shard_map/all_to_all | solution.py:178
  39.8 1.4 collective-permute-start
  41.2 1.5 collective-permute-start.1
  42.7 2.2 broadcast_in_dim.46
  45.8 1.4 add_reduce_fusion
  48.1 1.3 compare_convert_fusion
  49.4 1.4 reshape.407
  50.8 1.4 reduce-window.8
  54.7 21.8 %collective-permute-done = bf16[720,640]{1,0:T(8,128)(2,1)} collective-permute-done((bf16[720,640]{1,0:T(8,128)(2,1)S(1)}, bf16[720,640]{1,0:T(8,128)(2,1)}, u32[]{:S(2)}, u32[]{:S(2)}) %collective-permute-start) | collective-permute-done | bytes 921632 | tf_op jit(solution)/shard_map/ppermute | solution.py:18
  77.4 1.3 fusion.22
  78.7 2.3 constant_dynamic-update-slice_fusion.1
  80.9 2.3 constant_dynamic-update-slice_fusion
  83.2 30.7 %collective-permute-done.2 = bf16[720,640]{1,0:T(8,128)(2,1)} collective-permute-done((bf16[720,640]{1,0:T(8,128)(2,1)}, bf16[720,640]{1,0:T(8,128)(2,1)}, u32[]{:S(2)}, u32[]{:S(2)}) %collective-permute-start.2) | collective-permute-done | bytes 921632 | tf_op jit(solution)/shard_map/ppermute | solution.py:18
  114.0 2.2 constant_dynamic-update-slice_fusion.3
  116.2 2.5 reshape.388
  118.6 2.2 convolution_convert_fusion.1
  120.9 1.3 reshape.389
  122.2 5.3 %fusion.8 = f32[22,4,4,640]{3,0,2,1:T(8,128)S(1)} fusion(bf16[3,3,320,640]{3,2,1,0:T(8,128)(2,1)} %bitcast.49, bf16[22,8,8,320]{3,2,1,0:T(8,128)(2,1)S(1)} %reshape.389), kind=kOutput, calls=%fused_computation.27 | convolution fusion | flops 1090355200 | bytes 5488640 | tf_op jit(solution)/shard_map/conv_general_dilated | solution.py:31
  127.5 5.0 %multiply_reduce_fusion.2 = (f32[22,640]{1,0:T(8,128)S(1)}, f32[22,640]{1,0:T(8,128)S(1)}, f32[22,4,4,640]{3,0,2,1:T(8,128)S(1)}) fusion(f32[22,4]{0,1:T(4,128)S(1)} %fusion.23, f32[22,4,4,640]{3,0,2,1:T(8,128)S(1)} %fusion.8, bf16[3,3,320,640]{3,2,1,0:T(8,128)(2,1)} %bitcast.7, bf16[22,8,8,320]{3,2,1,0:T(8,128)(2,1)S(1)} %reshape.389), kind=kOutput, calls=%fused_computation.18 | convolution fusion | flops 1091228160 | bytes 6502752 | tf_op jit(solution)/shard_map/conv_general_dilated | solution.py:31
  138.1 6.6 %copy.64 = bf16[4,1440,320]{2,1,0:T(8,128)(2,1)} copy(bf16[4,1440,320]{1,2,0:T(8,128)(2,1)} %all-gather.8.cloned.1.call-done) | data formatting | bytes 7372800 | tf_op jit(solution)/shard_map/all_gather | solution.py:197
  144.7 1.6 multiply_convert_fusion.2
  146.7 1.3 copy-done.2
  147.9 1.4 copy-done
  149.3 11.1 %fusion.1 = bf16[22,8,8,320]{3,0,2,1:T(8,128)(2,1)} fusion(bf16[22,8,8,640]{3,0,2,1:T(8,128)(2,1)S(1)} %bitcast.42, bf16[3,3,640,320]{3,2,1,0:T(8,128)(2,1)S(1)} %bitcast.33, f32[22,8]{0,1:T(8,128)S(1)} %copy-done.19, bf16[22,8,8,320]{3,2,1,0:T(8,128)(2,1)S(1)} %copy-done.7), kind=kOutput, calls=%fused_computation.7 | convolution fusion | flops 4363223040 | bytes 7291584 | tf_op jit(solution)/shard_map/conv_general_dilated | solution.py:31
  160.4 18.2 %all-gather.10.cloned.1.call-done = bf16[4,1440,320]{1,2,0:T(8,128)(2,1)} async-done(((bf16[1,1440,320]{1,2,0:T(8,128)(2,1)}), bf16[4,1440,320]{1,2,0:T(8,128)(2,1)}) %all-gather.10.cloned.1.call-update) | async-done | bytes 3686416 | tf_op jit(solution)/shard_map/all_gather | solution.py:175
  178.6 6.3 %copy.67 = bf16[4,1440,320]{2,1,0:T(8,128)(2,1)} copy(bf16[4,1440,320]{1,2,0:T(8,128)(2,1)} %all-gather.10.cloned.1.call-done) | data formatting | bytes 7372800 | tf_op jit(solution)/shard_map/all_gather | solution.py:175
  185.2 1.9 copy-done.1
  187.2 12.5 %multiply_convert_fusion = bf16[22,8,8,320]{3,0,2,1:T(8,128)(2,1)S(1)} fusion(bf16[22,8,8,320]{3,0,2,1:T(8,128)(2,1)} %fusion.1, bf16[22,8,8,640]{3,0,2,1:T(8,128)(2,1)S(1)} %bitcast.44, bf16[3,3,640,320]{3,2,1,0:T(8,128)(2,1)S(1)} %bitcast.37, bf16[22,8,8,320]{3,2,1,0:T(8,128)(2,1)} %param.15, f32[22,8]{0,1:T(8,128)S(1)} %copy-done.19, ...), kind=kOutput, calls=%fused_computation.10 | convolution fusion | flops 4367278080 | bytes 9093824 | tf_op jit(solution)/shard_map/conv_general_dilated | solution.py:31
  199.7 10.7 %fusion.27 = f32[22,8,8,640]{3,0,2,1:T(8,128)} fusion(bf16[22,8,8,320]{3,0,2,1:T(8,128)(2,1)S(1)} %multiply_convert_fusion, bf16[3,3,640,320]{3,2,1,0:T(8,128)(2,1)S(1)} %bitcast.36), kind=kOutput, calls=%fused_computation.76 | convolution fusion | flops 4361420800 | bytes 8192000 | tf_op jit(solution)/shard_map/conv_general_dilated | solution.py:31
  210.5 2.5 reduce_sum.161
  216.1 1.2 reduce_sum.166
  218.2 1.4 broadcast_divide_fusion.1
  223.1 3.6 mul.227
  226.7 7.6 %mul.228 = f32[22,4,4,640]{3,2,1,0:T(4,128)} reshape(f32[22,16,32,20]{3,2,1,0:T(8,128)} %mul.227) | data formatting | bytes 1802240 | tf_op jit(solution)/shard_map/mul | solution.py:92
  234.3 6.4 %convolution_convert_fusion.2 = bf16[3,3,320,640]{3,2,1,0:T(8,128)(2,1)} fusion(bf16[22,8,8,320]{3,2,1,0:T(8,128)(2,1)S(1)} %copy-done.7, f32[22,4,4,640]{3,2,1,0:T(4,128)} %mul.228, f32[22,4,4,640]{3,0,2,1:T(8,128)S(1)} %fusion.8, f32[22,640]{1,0:T(8,128)S(1)} %copy-done.14, f32[22,640]{1,0:T(8,128)S(1)} %copy-done.15, f32[22,640]{1,0:T(8,128)S(1)} %copy-done.12, ...), kind=kOutput, calls=%fused_computation.4 | convolution fusion | flops 1095802880 | bytes 7516512 | tf_op jit(solution)/shard_map/conv_general_dilated | solution.py:43
  240.8 1.5 copy-done.3
  242.5 7.9 %convolution_convert_fusion.3 = bf16[3,3,640,320]{2,3,1,0:T(8,128)(2,1)} fusion(bf16[22,8,8,640]{3,0,2,1:T(8,128)(2,1)S(1)} %bitcast.43, bf16[22,8,8,320]{3,0,2,1:T(8,128)(2,1)S(1)} %copy-done.25), kind=kOutput, calls=%fused_computation.5 | convolution fusion | flops 4363264000 | bytes 6389760 | tf_op jit(solution)/shard_map/conv_general_dilated | solution.py:43
  250.4 7.9 %copy.71 = bf16[3,3,640,320]{3,2,1,0:T(8,128)(2,1)} copy(bf16[3,3,640,320]{2,3,1,0:T(8,128)(2,1)} %convolution_convert_fusion.3) | data formatting | bytes 7372800 | tf_op jit(solution)/shard_map/convert_element_type | solution.py:213
  258.4 25.7 %reduce-scatter.3.cloned.1.call-done = bf16[720,640]{1,0:T(8,128)(2,1)} async-done(((bf16[2880,640]{1,0:T(8,128)(2,1)}), bf16[720,640]{1,0:T(8,128)(2,1)}) %reduce-scatter.3.cloned.1.call-update) | async-done | bytes 921616 | tf_op jit(solution)/shard_map/reduce_scatter | solution.py:209
  284.1 50.7 %reduce-scatter.5.cloned.1.call-done = bf16[1440,320]{1,0:T(8,128)(2,1)} async-done(((bf16[5760,320]{1,0:T(8,128)(2,1)}), bf16[1440,320]{1,0:T(8,128)(2,1)}) %reduce-scatter.5.cloned.1.call-update) | async-done | bytes 921616 | tf_op jit(solution)/shard_map/reduce_scatter | solution.py:212
  336.0 109.8 %all-reduce.3.cloned.1.call-done = (bf16[1440,320]{1,0:T(8,128)(2,1)}, bf16[720,640]{1,0:T(8,128)(2,1)}) async-done(((bf16[1440,320]{1,0:T(8,128)(2,1)}, bf16[720,640]{1,0:T(8,128)(2,1)}), (bf16[1440,320]{1,0:T(8,128)(2,1)}, bf16[720,640]{1,0:T(8,128)(2,1)})) %all-reduce.3.cloned.1.call-update) | async-done | bytes 1843216 | tf_op jit(solution)/shard_map/psum | solution.py:218
  445.8 2.6 copy.73
  448.5 1.4 convert_element_type.153
  (125 shorter events, 26.3 us)
Async XLA Ops:
  7.2 14.9 %copy-start.5 = (bf16[22,8,8,320]{3,2,1,0:T(8,128)(2,1)S(1)}, bf16[22,8,8,320]{3,2,1,0:T(8,128)(2,1)}, u32[]{:S(2)}) copy-start(bf16[22,8,8,320]{3,2,1,0:T(8,128)(2,1)} %param.11) | copy-start | bytes 2703364
  7.2 115.0 %all-gather.6.cloned.1.call-start = ((), (), s32[]{:S(2)}) async-start(), calls=%async_computation.4 | async-start | bytes 4608000 | tf_op jit(solution)/shard_map/all_gather | solution.py:196
  7.9 130.2 %all-gather.8.cloned.1.call-start = ((), (), s32[]{:S(2)}) async-start(), calls=%async_computation.7 | async-start | bytes 4915200 | tf_op jit(solution)/shard_map/all_gather | solution.py:197
  11.8 19.7 %all-to-all-start = ((s32[32,1,2]{2,1,0:T(1,128)}), s32[32,1,2]{2,1,0:T(1,128)}, u32[]{:S(2)}, u32[]{:S(2)}) async-start(s32[32,1,2]{2,1,0:T(1,128)} %bitcast), calls=%async_computation | async-start | bytes 32768 | tf_op jit(solution)/shard_map/all_to_all | solution.py:179
  31.5 8.3 %copy-start.10 = (bf16[720,640]{1,0:T(8,128)(2,1)S(1)}, bf16[720,640]{1,0:T(8,128)(2,1)}, u32[]{:S(2)}) copy-start(bf16[720,640]{1,0:T(8,128)(2,1)} %param.18) | copy-start | bytes 2764804
  31.5 84.7 %all-to-all-start.1 = ((bf16[32,2,20480]{2,1,0:T(2,128)(2,1)}), bf16[32,2,20480]{2,1,0:T(2,128)(2,1)S(1)}, u32[]{:S(2)}, u32[]{:S(2)}) async-start(bf16[32,2,20480]{2,1,0:T(2,128)(2,1)} %reshape.387), calls=%async_computation.1 | async-start | bytes 5242880 | tf_op jit(solution)/shard_map/all_to_all | solution.py:178
  39.0 139.6 %all-gather.10.cloned.1.call-start = ((), (), s32[]{:S(2)}) async-start(), calls=%async_computation.8 | async-start | bytes 4915200 | tf_op jit(solution)/shard_map/all_gather | solution.py:175
  39.7 244.3 %reduce-scatter.3.cloned.1.call-start = ((), (), s32[]{:S(2)}) async-start(), calls=%async_computation.5 | async-start | bytes 4608000 | tf_op jit(solution)/shard_map/reduce_scatter | solution.py:209
  39.8 36.7 %collective-permute-start = (bf16[720,640]{1,0:T(8,128)(2,1)S(1)}, bf16[720,640]{1,0:T(8,128)(2,1)}, u32[]{:S(2)}, u32[]{:S(2)}) collective-permute-start(bf16[720,640]{1,0:T(8,128)(2,1)S(1)} %copy-done.10), channel_id=1, source_target_pairs={{0,1},{1,2},{2,3},{3,0},{4,5},{5,6},{6,7},{7,4},{8,9},{9,10},{10,1... | collective-permute-start | bytes 2764808 | tf_op jit(solution)/shard_map/ppermute | solution.py:18
  41.2 39.8 %collective-permute-start.1 = (bf16[720,640]{1,0:T(8,128)(2,1)S(1)}, bf16[720,640]{1,0:T(8,128)(2,1)}, u32[]{:S(2)}, u32[]{:S(2)}) collective-permute-start(bf16[720,640]{1,0:T(8,128)(2,1)S(1)} %copy-done.10), channel_id=1, source_target_pairs={{0,3},{1,0},{2,1},{3,2},{4,7},{5,4},{6,5},{7,6},{8,11},{9,8},{10,9... | collective-permute-start | bytes 2764808 | tf_op jit(solution)/shard_map/ppermute | solution.py:21
  54.0 22.7 %copy-start.20 = (s32[64]{0:T(128)}, s32[64]{0:T(128)S(1)}, u32[]{:S(2)}) copy-start(s32[64]{0:T(128)S(1)} %sub.103) | copy-start | bytes 772
  54.0 22.7 %copy-start.22 = (pred[64]{0:T(512)(128)(4,1)}, pred[64]{0:T(512)(128)(4,1)S(1)}, u32[]{:S(2)}) copy-start(pred[64]{0:T(512)(128)(4,1)S(1)} %broadcast_compare_fusion) | copy-start | bytes 196
  76.5 37.5 %collective-permute-start.2 = (bf16[720,640]{1,0:T(8,128)(2,1)}, bf16[720,640]{1,0:T(8,128)(2,1)}, u32[]{:S(2)}, u32[]{:S(2)}) collective-permute-start(bf16[720,640]{1,0:T(8,128)(2,1)} %collective-permute-done), channel_id=1, source_target_pairs={{0,1},{1,2},{2,3},{3,0},{4,5},{5,6},{6,7},{7,4},{8,9},{9,10},{10,1... | collective-permute-start | bytes 2764808 | tf_op jit(solution)/shard_map/ppermute | solution.py:18
  77.4 56.2 %copy-start.16 = (f32[22]{0:T(128)}, f32[22]{0:T(128)S(1)}, u32[]{:S(2)}) copy-start(f32[22]{0:T(128)S(1)} %broadcast_multiply_fusion.1) | copy-start | bytes 268
  116.1 2.5 copy-start.21
  116.2 2.5 copy-start.23
  122.1 5.4 %copy-start.6 = (bf16[22,8,8,320]{3,2,1,0:T(8,128)(2,1)}, bf16[22,8,8,320]{3,2,1,0:T(8,128)(2,1)S(1)}, u32[]{:S(2)}) copy-start(bf16[22,8,8,320]{3,2,1,0:T(8,128)(2,1)S(1)} %reshape.389) | copy-start | bytes 2703364
  134.1 2.1 copy-start.8
  134.1 1.9 copy-start.17
  134.5 2.7 copy-start.13
  144.7 3.3 copy-start.7
  146.3 3.0 copy-start
  146.3 3.0 copy-start.19
  146.6 1.3 copy-start.2
  184.9 2.3 copy-start.1
  185.0 14.7 %slice-start = ((s8[4423680]{0:T(1024)(128)(4,1)}), s8[4194304]{0:T(1024)(128)(4,1)S(1)}, s32[]{:S(2)}) async-start(s8[4423680]{0:T(1024)(128)(4,1)} %bitcast.34), calls=%async_computation.10 | async-start | bytes 8388608
  187.2 12.6 %slice-start.1 = ((s8[4423680]{0:T(1024)(128)(4,1)}), s8[229376]{0:T(1024)(128)(4,1)S(1)}, s32[]{:S(2)}) async-start(s8[4423680]{0:T(1024)(128)(4,1)} %bitcast.34), calls=%async_computation.11 | async-start | bytes 458752
  199.7 10.8 %copy-start.24 = (bf16[22,8,8,320]{3,0,2,1:T(8,128)(2,1)}, bf16[22,8,8,320]{3,0,2,1:T(8,128)(2,1)S(1)}, u32[]{:S(2)}) copy-start(bf16[22,8,8,320]{3,0,2,1:T(8,128)(2,1)S(1)} %multiply_convert_fusion) | copy-start | bytes 2703364
  210.5 2.5 copy-start.9
  210.5 2.5 copy-start.12
  213.0 5.2 %copy-start.18 = (f32[22]{0:T(128)S(1)}, f32[22]{0:T(128)}, u32[]{:S(2)}) copy-start(f32[22]{0:T(128)} %copy-done.16) | copy-start | bytes 268
  226.7 7.6 %copy-start.14 = (f32[22,640]{1,0:T(8,128)S(1)}, f32[22,640]{1,0:T(8,128)}, u32[]{:S(2)}) copy-start(f32[22,640]{1,0:T(8,128)} %mul.253) | copy-start | bytes 168964
  226.7 7.6 %copy-start.15 = (f32[22,640]{1,0:T(8,128)S(1)}, f32[22,640]{1,0:T(8,128)}, u32[]{:S(2)}) copy-start(f32[22,640]{1,0:T(8,128)} %sub.123) | copy-start | bytes 168964
  240.7 1.5 copy-start.3
  240.7 1.9 copy-start.25
  240.7 94.1 %reduce-scatter.5.cloned.1.call-start = ((), (), s32[]{:S(2)}) async-start(), calls=%async_computation.6 | async-start | bytes 5529600 | tf_op jit(solution)/shard_map/reduce_scatter | solution.py:212
  258.3 76.5 %copy-start.4 = (bf16[22,8,8,320]{3,0,2,1:T(8,128)(2,1)S(1)}, bf16[22,8,8,320]{3,0,2,1:T(8,128)(2,1)}, u32[]{:S(2)}) copy-start(bf16[22,8,8,320]{3,0,2,1:T(8,128)(2,1)} %fusion.1) | copy-start | bytes 2703364
  258.3 187.5 %all-reduce.3.cloned.1.call-start = ((), (), s32[]{:S(2)}) async-start(), calls=%async_computation.9 | async-start | bytes 4055040 | tf_op jit(solution)/shard_map/psum | solution.py:218
  445.8 2.6 copy-start.11
Sparse Core Ops, SparseCore 0:
  9.6 59.3 all-gather.5
  70.7 61.5 all-gather.7
  134.0 44.5 all-gather.9
  240.8 43.1 reduce-scatter.2
  286.3 48.4 reduce-scatter.4
  338.1 107.6 all-reduce.2
